TPU v7x, 32 devices: a whole 2x2x4 slice. The times are simulated.
32 devices in a mesh: gz: 4 (over x, core), gy: 4 (over z), gx: 2 (over y).
Axes of the slice: x: 2, y: 2, z: 4, core: 2. Of those that a mesh axis runs over, the one named last changes fastest.
Arguments:
- volume: bfloat16 [32, 4, 32, 384], P('gz', 'gy', 'gx'), may hold values from -80 to 80
- cotangent: bfloat16 [32, 4, 32, 384], P('gz', 'gy', 'gx'), may hold values from -6 to 6
- w_project: bfloat16 [3, 384, 1152], P(None, 'gy', ('gz', 'gx')), may hold values from -0.3125 to 0.3125
- w_output: bfloat16 [3, 384, 384], P(None, 'gy', ('gz', 'gx')), may hold values from -0.3125 to 0.3125
Outputs:
- grad_volume: bfloat16 [32, 4, 32, 384], P('gz', 'gy', 'gx')
All inputs are finite; a program needn't handle non-finite values.
Results may differ from a plain program's by a relative error of at most 0.015.
Values may be sent and summed in bfloat16 or wider, within the bound.
No kernel may reach another device: no remote copies, remote signals or barrier semaphores. Data moves between devices by JAX's collectives and lax.ppermute only.
A program may use at most 64 MiB of HBM per device.

v0:
```python
import jax
import jax.numpy as jnp
from jax import lax
from jax.sharding import PartitionSpec as P

HEADS = 6
ALL = ("gz", "gy", "gx")


def head_norm(vector):
    return (vector * lax.rsqrt(jnp.mean(vector * vector, axis=-1, keepdims=True) + 1e-06)).astype(
        jnp.bfloat16
    )


def sublayer(line_rows, w_inner, w_outer):
    feat_len = line_rows.shape[-1]
    head_size = feat_len // HEADS
    stream = line_rows.astype(jnp.float32)
    normed = (stream * lax.rsqrt(jnp.mean(stream * stream, axis=-1, keepdims=True) + 1e-06)).astype(
        jnp.bfloat16
    )
    packed = jnp.dot(normed, w_inner, preferred_element_type=jnp.float32)
    head_shape = line_rows.shape[:3] + (HEADS, head_size)
    queries = head_norm(packed[..., :feat_len].reshape(head_shape))
    key_part = head_norm(packed[..., feat_len : 2 * feat_len].reshape(head_shape))
    value_part = packed[..., 2 * feat_len :].reshape(head_shape).astype(jnp.bfloat16)
    scores = jnp.einsum(
        "plqhe,pkqhe->pqhlk", queries, key_part, preferred_element_type=jnp.float32
    ) * head_size ** (-0.5)
    powers = jnp.exp(scores)
    attn_weights = (powers / jnp.sum(powers, axis=-1, keepdims=True)).astype(jnp.bfloat16)
    mixed_out = jnp.einsum(
        "pqhlk,pkqhe->plqhe", attn_weights, value_part, preferred_element_type=jnp.float32
    )
    mixed_out = mixed_out.astype(jnp.bfloat16).reshape(line_rows.shape)
    update = jnp.dot(mixed_out, w_outer, preferred_element_type=jnp.float32)
    return (stream + update).astype(jnp.bfloat16)


def full_weights(w_project, w_output, index, sizes):
    nz, ny, nx = sizes
    proj, outp = (w_project[index], w_output[index])
    din, dproj = proj.shape
    cat = jnp.concatenate([proj, outp], axis=1)
    got = lax.all_gather(cat, ALL, axis=0, tiled=False)
    got = got.reshape(nz, ny, nx, din, cat.shape[1])
    got = jnp.transpose(got, (1, 3, 0, 2, 4)).reshape(ny * din, nz * nx, cat.shape[1])
    w_inner = got[:, :, :dproj].reshape(ny * din, nz * nx * dproj)
    w_outer = got[:, :, dproj:].reshape(ny * din, -1)
    return (w_inner, w_outer)


def depth_fn(member, w_inner, w_outer):
    depth_len, row_len, rest_len, feat_len = member.shape
    flat_lines = member.reshape(1, depth_len, row_len * rest_len, feat_len)
    return sublayer(flat_lines, w_inner, w_outer).reshape(member.shape)


def plane_fn(plane, w_row, w_col):
    after_rows = sublayer(plane[None], *w_row)[0]
    return sublayer(after_rows[:, :, None, :], *w_col)[:, :, 0, :]


def to_planes(depth_lines, sizes):
    nz, ny, nx = sizes
    z_len, yl, kx, feat = depth_lines.shape
    got = lax.all_to_all(depth_lines, ALL, 0, 0, tiled=True)
    got = got.reshape(nz, ny, nx, yl, kx, feat)
    return jnp.transpose(got, (1, 3, 2, 0, 4, 5)).reshape(ny * yl, nx * nz * kx, feat)


def from_planes(plane, sizes):
    nz, ny, nx = sizes
    rows, cols, feat = plane.shape
    yl, kx = (rows // ny, cols // (nx * nz))
    parts = plane.reshape(ny, yl, nx, nz, kx, feat)
    parts = jnp.transpose(parts, (3, 0, 2, 1, 4, 5)).reshape(nz * ny * nx, yl, kx, feat)
    return lax.all_to_all(parts, ALL, 0, 0, tiled=True)


def block_to_plane(block, sizes):
    nz, ny, nx = sizes
    zl, yl, xl, feat = block.shape
    got = lax.all_to_all(block, ("gy", "gx"), 0, 0, tiled=True)
    got = got.reshape(ny, nx, yl, xl, feat)
    return jnp.transpose(got, (0, 2, 1, 3, 4)).reshape(ny * yl, nx * xl, feat)


def local(volume, cotangent, w_project, w_output, sizes):
    w_depth = full_weights(w_project, w_output, 0, sizes)
    w_row = full_weights(w_project, w_output, 1, sizes)
    w_col = full_weights(w_project, w_output, 2, sizes)
    depth_act = lax.all_to_all(volume, "gz", 2, 0, tiled=True)
    cot_plane = block_to_plane(cotangent, sizes)
    field_one, depth_pullback = jax.vjp(lambda m: depth_fn(m, *w_depth), depth_act)
    plane_one = to_planes(field_one, sizes)
    _, plane_pullback = jax.vjp(lambda p: plane_fn(p, w_row, w_col), plane_one)
    grad_plane = plane_pullback(cot_plane)[0]
    grad_one = from_planes(grad_plane, sizes)
    grad_zero = depth_pullback(grad_one)[0]
    return lax.all_to_all(grad_zero, "gz", 0, 2, tiled=True)


def along_rows(member, w_inner, w_outer):
    return sublayer(member, w_inner, w_outer)


def along_columns(member, w_inner, w_outer):
    depth_len, row_len, col_len, feat_len = member.shape
    flat_lines = member.reshape(depth_len * row_len, col_len, 1, feat_len)
    return sublayer(flat_lines, w_inner, w_outer).reshape(member.shape)


def line_swap(stacked, axis, split_axis, concat_axis):
    return lax.all_to_all(stacked, axis, split_axis=split_axis, concat_axis=concat_axis, tiled=True)


def local_general(volume, cotangent, w_project, w_output, sizes):
    w_depth = full_weights(w_project, w_output, 0, sizes)
    w_row = full_weights(w_project, w_output, 1, sizes)
    w_col = full_weights(w_project, w_output, 2, sizes)

    def row_fn(member):
        return along_rows(member, *w_row)

    def column_fn(member):
        return along_columns(member, *w_col)

    depth_act = line_swap(volume, "gz", 2, 0)
    field_one, depth_pullback = jax.vjp(lambda m: depth_fn(m, *w_depth), depth_act)
    field_one = line_swap(field_one, "gz", 0, 2)
    row_act = line_swap(field_one, "gy", 2, 1)
    field_two, row_pullback = jax.vjp(row_fn, row_act)
    field_two = line_swap(field_two, "gy", 1, 2)
    paired = line_swap(jnp.stack([cotangent, field_two]), "gx", 1, 3)
    _, column_pullback = jax.vjp(column_fn, paired[1])
    grad_two = line_swap(column_pullback(paired[0])[0], "gx", 2, 0)
    grad_one = line_swap(row_pullback(line_swap(grad_two, "gy", 2, 1))[0], "gy", 1, 2)
    grad_zero = depth_pullback(line_swap(grad_one, "gz", 2, 0))[0]
    return line_swap(grad_zero, "gz", 0, 2)


def solution(mesh):
    sizes = (mesh.shape["gz"], mesh.shape["gy"], mesh.shape["gx"])

    def body(volume, *rest):
        one_depth = volume.shape[0] * sizes[0] == mesh.size
        return (local if one_depth else local_general)(volume, *rest, sizes)

    return jax.shard_map(
        body,
        mesh=mesh,
        in_specs=(
            P("gz", "gy", "gx", None),
            P("gz", "gy", "gx", None),
            P(None, "gy", ("gz", "gx")),
            P(None, "gy", ("gz", "gx")),
        ),
        out_specs=P("gz", "gy", "gx", None),
        check_vma=False,
    )
```

profile of v0, /device:TPU:0, one launch (start us, length us, event | category | flops | bytes accessed | tf_op | source)
XLA Modules:
  0.0 310.3 jit_solution(6159842277848257346)
XLA Ops:
  11.9 8.3 %all_to_all.42 = bf16[8,1,16,384]{3,0,1,2:T(8,128)(2,1)S(1)} all-to-all(bf16[8,1,16,384]{3,0,1,2:T(8,128)(2,1)S(1)} %copy.516), channel_id=1, replica_groups=mesh['gz'=4,'gy'=4,'gx'=2] {'gz'}, dimensions={2} | all-to-all | bytes 196608 | tf_op jit(solution)/shard_map/all_to_all | solution.py:94
  20.3 5.8 %all-to-all-start = ((bf16[8,1,16,384]{3,2,1,0:T(8,128)(2,1)}), bf16[8,1,16,384]{3,2,1,0:T(8,128)(2,1)S(1)}, u32[]{:S(2)}, u32[]{:S(2)}) async-start(bf16[8,1,16,384]{3,2,1,0:T(8,128)(2,1)} %param.5), calls=%async_computation | async-start | bytes 196608 | tf_op jit(solution)/shard_map/all_to_all | solution.py:85
  26.9 41.2 %all-gather.9.cloned.1.call-done = bf16[3072,192]{1,0:T(8,128)(2,1)} async-done(((bf16[96,192]{1,0:T(8,128)(2,1)}), bf16[3072,192]{1,0:T(8,128)(2,1)}) %all-gather.9.cloned.1.call-update) | async-done | bytes 1179664 | tf_op jit(solution)/shard_map/all_gather | solution.py:46
  68.1 2.8 copy.522
  85.7 39.3 %all-gather.11.cloned.1.call-done = bf16[3072,192]{1,0:T(8,128)(2,1)} async-done(((bf16[96,192]{1,0:T(8,128)(2,1)}), bf16[3072,192]{1,0:T(8,128)(2,1)}) %all-gather.11.cloned.1.call-update) | async-done | bytes 1179664 | tf_op jit(solution)/shard_map/all_gather | solution.py:46
  125.0 2.8 copy.538
  129.7 52.1 %all-gather.7.cloned.1.call-done = bf16[3072,192]{1,0:T(8,128)(2,1)} async-done(((bf16[96,192]{1,0:T(8,128)(2,1)}), bf16[3072,192]{1,0:T(8,128)(2,1)}) %all-gather.7.cloned.1.call-update) | async-done | bytes 1179664 | tf_op jit(solution)/shard_map/all_gather | solution.py:46
  181.9 2.8 copy.514
  184.7 1.9 reshape.948
  191.3 3.7 %all-to-all-start.2 = ((bf16[32,1,4,384]{3,2,1,0:T(4,128)(2,1)}), bf16[32,1,4,384]{3,2,1,0:T(4,128)(2,1)S(1)}, u32[]{:S(2)}, u32[]{:S(2)}) async-start(bf16[32,1,4,384]{3,2,1,0:T(4,128)(2,1)} %copy.534), calls=%async_computation.2 | async-start | bytes 196608 | tf_op jit(solution)/shard_map/all_to_all | solution.py:68
  196.2 6.3 %all-to-all-done.2 = bf16[32,1,4,384]{3,2,1,0:T(4,128)(2,1)S(1)} async-done(((bf16[32,1,4,384]{3,2,1,0:T(4,128)(2,1)}), bf16[32,1,4,384]{3,2,1,0:T(4,128)(2,1)S(1)}, u32[]{:S(2)}, u32[]{:S(2)}) %all-to-all-start.2) | async-done | bytes 98336 | tf_op jit(solution)/shard_map/all_to_all | solution.py:68
  221.7 1.8 reshape.969
  227.4 1.9 reshape.973
  229.3 1.9 multiply_reduce_fusion.1
  234.7 1.8 reshape.972
  236.6 1.9 reshape.975
  238.4 1.9 multiply_reduce_fusion
  243.9 1.8 reshape.974
  261.9 1.9 reshape.977
  266.2 1.9 reshape.978
  271.1 2.0 fusion.14
  281.2 2.6 all-to-all-start.3
  283.8 7.6 %all-to-all-done.3 = bf16[32,1,4,384]{3,2,1,0:T(4,128)(2,1)S(1)} async-done(((bf16[32,1,4,384]{3,2,1,0:T(4,128)(2,1)}), bf16[32,1,4,384]{3,2,1,0:T(4,128)(2,1)S(1)}, u32[]{:S(2)}, u32[]{:S(2)}) %all-to-all-start.3) | async-done | bytes 98336 | tf_op jit(solution)/shard_map/all_to_all | solution.py:79
  296.4 6.7 %all_to_all.43 = bf16[32,1,4,384]{3,2,1,0:T(4,128)(2,1)S(1)} all-to-all(bf16[32,1,4,384]{3,2,1,0:T(4,128)(2,1)S(1)} %copy.626), channel_id=1, replica_groups=mesh['gz'=4,'gy'=4,'gx'=2] {'gz'}, dimensions={0} | all-to-all | bytes 196608 | tf_op jit(solution)/shard_map/all_to_all | solution.py:102
  (300 shorter events, 93.3 us)
Async XLA Ops:
  6.5 61.5 %all-gather.9.cloned.1.call-start = ((), (), s32[]{:S(2)}) async-start(), calls=%async_computation.6 | async-start | bytes 1622016 | tf_op jit(solution)/shard_map/all_gather | solution.py:46
  9.0 115.9 %all-gather.11.cloned.1.call-start = ((), (), s32[]{:S(2)}) async-start(), calls=%async_computation.7 | async-start | bytes 1622016 | tf_op jit(solution)/shard_map/all_gather | solution.py:46
  10.0 171.8 %all-gather.7.cloned.1.call-start = ((), (), s32[]{:S(2)}) async-start(), calls=%async_computation.5 | async-start | bytes 1622016 | tf_op jit(solution)/shard_map/all_gather | solution.py:46
  20.3 170.1 %copy-start.11 = (bf16[8,1,16,384]{3,0,1,2:T(8,128)(2,1)}, bf16[8,1,16,384]{3,0,1,2:T(8,128)(2,1)S(1)}, u32[]{:S(2)}) copy-start(bf16[8,1,16,384]{3,0,1,2:T(8,128)(2,1)S(1)} %all_to_all.42) | copy-start | bytes 294916
  20.3 171.1 %all-to-all-start = ((bf16[8,1,16,384]{3,2,1,0:T(8,128)(2,1)}), bf16[8,1,16,384]{3,2,1,0:T(8,128)(2,1)S(1)}, u32[]{:S(2)}, u32[]{:S(2)}) async-start(bf16[8,1,16,384]{3,2,1,0:T(8,128)(2,1)} %param.5), calls=%async_computation | async-start | bytes 196608 | tf_op jit(solution)/shard_map/all_to_all | solution.py:85
  74.0 9.7 %copy-start = (f32[1,32,4,6,64]{4,3,1,2,0:T(8,128)}, f32[1,32,4,6,64]{4,3,1,2,0:T(8,128)S(1)}, u32[]{:S(2)}) copy-start(f32[1,32,4,6,64]{4,3,1,2,0:T(8,128)S(1)} %reshape.958) | copy-start | bytes 589828
  83.9 41.0 %copy-start.16 = (f32[4,6,32,32]{2,3,1,0:T(8,128)}, f32[4,6,32,32]{2,3,1,0:T(8,128)S(1)}, u32[]{:S(2)}) copy-start(f32[4,6,32,32]{2,3,1,0:T(8,128)S(1)} %get-tuple-element.26) | copy-start | bytes 294916
  84.0 43.8 %copy-start.53 = (f32[4,6,32]{2,1,0:T(8,128)}, f32[4,6,32]{2,1,0:T(8,128)S(1)}, u32[]{:S(2)}) copy-start(f32[4,6,32]{2,1,0:T(8,128)S(1)} %get-tuple-element.25) | copy-start | bytes 9220
  186.6 3.5 %copy-start.38 = (bf16[1,32,4,6,64]{4,1,3,2,0:T(8,128)(2,1)S(1)}, bf16[1,32,4,6,64]{4,1,3,2,0:T(8,128)(2,1)}, u32[]{:S(2)}) copy-start(bf16[1,32,4,6,64]{4,1,3,2,0:T(8,128)(2,1)} %fusion.6) | copy-start | bytes 294916
  186.6 3.8 %copy-start.9 = (bf16[384,8,48]{0,2,1:T(8,128)(2,1)S(1)}, bf16[384,8,48]{0,2,1:T(8,128)(2,1)}, u32[]{:S(2)}) copy-start(bf16[384,8,48]{0,2,1:T(8,128)(2,1)} %slice.91) | copy-start | bytes 884740
  191.3 13.1 %copy-start.29 = (bf16[8,1,16,384]{3,2,1,0:T(8,128)(2,1)}, bf16[8,1,16,384]{3,2,1,0:T(8,128)(2,1)S(1)}, u32[]{:S(2)}) copy-start(bf16[8,1,16,384]{3,2,1,0:T(8,128)(2,1)S(1)} %all-to-all-done) | copy-start | bytes 294916
  191.3 11.1 %all-to-all-start.2 = ((bf16[32,1,4,384]{3,2,1,0:T(4,128)(2,1)}), bf16[32,1,4,384]{3,2,1,0:T(4,128)(2,1)S(1)}, u32[]{:S(2)}, u32[]{:S(2)}) async-start(bf16[32,1,4,384]{3,2,1,0:T(4,128)(2,1)} %copy.534), calls=%async_computation.2 | async-start | bytes 196608 | tf_op jit(solution)/shard_map/all_to_all | solution.py:68
  253.1 4.9 %copy-start.47 = (f32[4,32,6]{1,0,2:T(4,128)S(1)}, f32[4,32,6]{1,0,2:T(4,128)}, u32[]{:S(2)}) copy-start(f32[4,32,6]{1,0,2:T(4,128)} %copy.551) | copy-start | bytes 9220
  258.8 5.0 %copy-start.52 = (f32[4,32,6]{1,2,0:T(8,128)S(1)}, f32[4,32,6]{1,2,0:T(8,128)}, u32[]{:S(2)}) copy-start(f32[4,32,6]{1,2,0:T(8,128)} %copy.570) | copy-start | bytes 9220
  265.1 4.6 %copy-start.59 = (f32[4,32]{1,0:T(4,128)S(1)}, f32[4,32]{1,0:T(4,128)}, u32[]{:S(2)}) copy-start(f32[4,32]{1,0:T(4,128)} %copy-done.58) | copy-start | bytes 1540
  265.2 4.6 %copy-start.57 = (f32[4,32]{1,0:T(4,128)S(1)}, f32[4,32]{1,0:T(4,128)}, u32[]{:S(2)}) copy-start(f32[4,32]{1,0:T(4,128)} %copy-done.56) | copy-start | bytes 1540
  269.7 3.4 %copy-start.15 = (f32[32,6,4,4]{2,3,1,0:T(4,128)S(1)}, f32[32,6,4,4]{2,3,1,0:T(4,128)}, u32[]{:S(2)}) copy-start(f32[32,6,4,4]{2,3,1,0:T(4,128)} %copy-done.14) | copy-start | bytes 36868
  269.7 3.4 %copy-start.40 = (f32[32,6,4]{2,1,0:T(8,128)S(1)}, f32[32,6,4]{2,1,0:T(8,128)}, u32[]{:S(2)}) copy-start(f32[32,6,4]{2,1,0:T(8,128)} %multiply_divide_fusion) | copy-start | bytes 9220
  269.9 4.9 %copy-start.19 = (f32[32,6,4]{2,1,0:T(8,128)S(1)}, f32[32,6,4]{2,1,0:T(8,128)}, u32[]{:S(2)}) copy-start(f32[32,6,4]{2,1,0:T(8,128)} %copy-done.18) | copy-start | bytes 9220
  279.9 3.9 %copy-start.54 = (f32[4,6,32]{2,1,0:T(8,128)S(1)}, f32[4,6,32]{2,1,0:T(8,128)}, u32[]{:S(2)}) copy-start(f32[4,6,32]{2,1,0:T(8,128)} %copy-done.53) | copy-start | bytes 9220
  279.9 11.5 %copy-start.10 = (bf16[384,8,48]{0,2,1:T(8,128)(2,1)S(1)}, bf16[384,8,48]{0,2,1:T(8,128)(2,1)}, u32[]{:S(2)}) copy-start(bf16[384,8,48]{0,2,1:T(8,128)(2,1)} %slice.91) | copy-start | bytes 884740
  280.0 11.9 %copy-start.17 = (f32[4,6,32,32]{2,3,1,0:T(8,128)S(1)}, f32[4,6,32,32]{2,3,1,0:T(8,128)}, u32[]{:S(2)}) copy-start(f32[4,6,32,32]{2,3,1,0:T(8,128)} %copy-done.16) | copy-start | bytes 294916
  280.5 11.5 %copy-start.21 = (bf16[32,4,6,64]{3,2,0,1:T(8,128)(2,1)S(1)}, bf16[32,4,6,64]{3,2,0,1:T(8,128)(2,1)}, u32[]{:S(2)}) copy-start(bf16[32,4,6,64]{3,2,0,1:T(8,128)(2,1)} %convert_element_type.403) | copy-start | bytes 294916
  281.2 10.2 %all-to-all-start.3 = ((bf16[32,1,4,384]{3,2,1,0:T(4,128)(2,1)}), bf16[32,1,4,384]{3,2,1,0:T(4,128)(2,1)S(1)}, u32[]{:S(2)}, u32[]{:S(2)}) async-start(bf16[32,1,4,384]{3,2,1,0:T(4,128)(2,1)} %bitcast.70), calls=%async_computation.3 | async-start | bytes 196608 | tf_op jit(solution)/shard_map/all_to_all | solution.py:79
  (43 other events, 63.8 us)
Sparse Core Ops, SparseCore 0:
  10.2 57.8 all-gather.8
  71.0 53.9 all-gather.10
  127.9 53.9 all-gather.6
where the time goes:
time: 312 us; the launch traced here: 310 us
  waiting for transfers between devices  146 us (47%)
  local copies, waits for them, and re-layouts  76.9 us (25%)
  other arithmetic  27.8 us (9%)
  matrix products  17.5 us (6%)
  blocking collectives  15 us (5%)
  between operations  14.4 us (5%)
  starting transfers between devices  12.2 us (4%)
    all_gather x3, waiting for transfers between devices, full_weights(): got = lax.all_gather(cat, ALL, axis=0, tiled=False)  133 us
    reshape x3, local copies, waits for them, and re-layouts, full_weights(): got = got.reshape(nz, ny, nx, din, cat.shape[1])  8.39 us
    all_to_all x1, blocking collectives, local(): depth_act = lax.all_to_all(volume, 'gz', 2, 0, tiled=True)  8.33 us
    reshape x9, local copies, waits for them, and re-layouts, sublayer(): key_part = head_norm(packed[..., feat_len:2 * feat_len].reshape(head_shape))  8.21 us
    rsqrt x12, local copies, waits for them, and re-layouts, head_norm(): lax.rsqrt(jnp.mean(vector * vector, axis=-1, keepdims=True) + 1e-06)  8.07 us
    all_to_all x1, waiting for transfers between devices, from_planes(): return lax.all_to_all(parts, ALL, 0, 0, tiled=True)  7.56 us
    reshape x9, local copies, waits for them, and re-layouts, sublayer(): queries = head_norm(packed[..., :feat_len].reshape(head_shape))  7.11 us
    all_to_all x1, blocking collectives, local(): return lax.all_to_all(grad_zero, 'gz', 0, 2, tiled=True)  6.67 us
  transfers between devices with their start and end apart: 6, of which 5 were waited for; matrix products, arithmetic and copies ran while one was open for 12% of the time, Pallas kernels for 0%

commit v1 on v0

--- a/solution.py
+++ b/solution.py
@@ -5,6 +5,14 @@
 
 HEADS = 6
 ALL = ("gz", "gy", "gx")
+
+
+def _bind_table(s0):
+    b_now = jnp.concatenate(
+        jax.lax.all_to_all(jnp.stack(jnp.split(s0, jax.lax.psum(1, "gz"), axis=0)), "gz", 0, 0),
+        axis=2,
+    )
+    return b_now
 
 
 def head_norm(vector):
@@ -99,7 +107,7 @@
     grad_plane = plane_pullback(cot_plane)[0]
     grad_one = from_planes(grad_plane, sizes)
     grad_zero = depth_pullback(grad_one)[0]
-    return lax.all_to_all(grad_zero, "gz", 0, 2, tiled=True)
+    return _bind_table(grad_zero)
 
 
 def along_rows(member, w_inner, w_outer):

time: 312 us -> 312 us (level)
  no operation moved by 1% of the time
where the time goes in v1:
time: 312 us; the launch traced here: 310 us
  waiting for transfers between devices  147 us (47%)
  local copies, waits for them, and re-layouts  76.6 us (25%)
  other arithmetic  27.8 us (9%)
  matrix products  17.5 us (6%)
  blocking collectives  15 us (5%)
  between operations  14.4 us (5%)
  starting transfers between devices  12.2 us (4%)
    all_gather x3, waiting for transfers between devices, full_weights(): got = lax.all_gather(cat, ALL, axis=0, tiled=False)  133 us
    reshape x3, local copies, waits for them, and re-layouts, full_weights(): got = got.reshape(nz, ny, nx, din, cat.shape[1])  8.39 us
    all_to_all x1, blocking collectives, local(): depth_act = lax.all_to_all(volume, 'gz', 2, 0, tiled=True)  8.33 us
    reshape x9, local copies, waits for them, and re-layouts, sublayer(): key_part = head_norm(packed[..., feat_len:2 * feat_len].reshape(head_shape))  8.21 us
    rsqrt x12, local copies, waits for them, and re-layouts, head_norm(): lax.rsqrt(jnp.mean(vector * vector, axis=-1, keepdims=True) + 1e-06)  8.03 us
    all_to_all x1, waiting for transfers between devices, from_planes(): return lax.all_to_all(parts, ALL, 0, 0, tiled=True)  7.56 us
    reshape x9, local copies, waits for them, and re-layouts, sublayer(): queries = head_norm(packed[..., :feat_len].reshape(head_shape))  7.11 us
    all_to_all x1, blocking collectives, _bind_table(): jax.lax.all_to_all(jnp.stack(jnp.split(s0, jax.lax.psum(1, 'gz'), axis=0)...  6.67 us
  transfers between devices with their start and end apart: 6, of which 5 were waited for; matrix products, arithmetic and copies ran while one was open for 12% of the time, Pallas kernels for 0%

profile of v1, /device:TPU:0, one launch (start us, length us, event | category | flops | bytes accessed | tf_op | source)
XLA Modules:
  0.0 310.0 jit_solution(10911965370553076256)
XLA Ops:
  11.9 8.3 %all_to_all.29 = bf16[8,1,16,384]{3,0,1,2:T(8,128)(2,1)S(1)} all-to-all(bf16[8,1,16,384]{3,0,1,2:T(8,128)(2,1)S(1)} %copy.512), channel_id=1, replica_groups=mesh['gz'=4,'gy'=4,'gx'=2] {'gz'}, dimensions={2} | all-to-all | bytes 196608 | tf_op jit(solution)/shard_map/all_to_all | solution.py:102
  20.3 5.8 %all-to-all-start = ((bf16[8,1,16,384]{3,2,1,0:T(8,128)(2,1)}), bf16[8,1,16,384]{3,2,1,0:T(8,128)(2,1)S(1)}, u32[]{:S(2)}, u32[]{:S(2)}) async-start(bf16[8,1,16,384]{3,2,1,0:T(8,128)(2,1)} %param.5), calls=%async_computation | async-start | bytes 196608 | tf_op jit(solution)/shard_map/all_to_all | solution.py:93
  26.9 41.2 %all-gather.9.cloned.1.call-done = bf16[3072,192]{1,0:T(8,128)(2,1)} async-done(((bf16[96,192]{1,0:T(8,128)(2,1)}), bf16[3072,192]{1,0:T(8,128)(2,1)}) %all-gather.9.cloned.1.call-update) | async-done | bytes 1179664 | tf_op jit(solution)/shard_map/all_gather | solution.py:54
  68.1 2.8 copy.518
  85.7 39.3 %all-gather.11.cloned.1.call-done = bf16[3072,192]{1,0:T(8,128)(2,1)} async-done(((bf16[96,192]{1,0:T(8,128)(2,1)}), bf16[3072,192]{1,0:T(8,128)(2,1)}) %all-gather.11.cloned.1.call-update) | async-done | bytes 1179664 | tf_op jit(solution)/shard_map/all_gather | solution.py:54
  125.0 2.8 copy.534
  129.7 52.1 %all-gather.7.cloned.1.call-done = bf16[3072,192]{1,0:T(8,128)(2,1)} async-done(((bf16[96,192]{1,0:T(8,128)(2,1)}), bf16[3072,192]{1,0:T(8,128)(2,1)}) %all-gather.7.cloned.1.call-update) | async-done | bytes 1179664 | tf_op jit(solution)/shard_map/all_gather | solution.py:54
  181.9 2.8 copy.510
  184.7 1.9 reshape.959
  191.3 3.7 %all-to-all-start.2 = ((bf16[32,1,4,384]{3,2,1,0:T(4,128)(2,1)}), bf16[32,1,4,384]{3,2,1,0:T(4,128)(2,1)S(1)}, u32[]{:S(2)}, u32[]{:S(2)}) async-start(bf16[32,1,4,384]{3,2,1,0:T(4,128)(2,1)} %copy.530), calls=%async_computation.2 | async-start | bytes 196608 | tf_op jit(solution)/shard_map/all_to_all | solution.py:76
  196.1 6.3 %all-to-all-done.2 = bf16[32,1,4,384]{3,2,1,0:T(4,128)(2,1)S(1)} async-done(((bf16[32,1,4,384]{3,2,1,0:T(4,128)(2,1)}), bf16[32,1,4,384]{3,2,1,0:T(4,128)(2,1)S(1)}, u32[]{:S(2)}, u32[]{:S(2)}) %all-to-all-start.2) | async-done | bytes 98336 | tf_op jit(solution)/shard_map/all_to_all | solution.py:76
  227.3 1.9 reshape.984
  229.2 1.9 multiply_reduce_fusion.1
  234.6 1.8 reshape.983
  236.5 1.9 reshape.986
  238.4 1.9 multiply_reduce_fusion
  243.8 1.8 reshape.985
  255.3 1.8 reshape.987
  261.7 1.9 reshape.988
  266.1 1.9 reshape.989
  270.9 2.0 fusion.14
  281.0 2.6 all-to-all-start.3
  283.7 7.6 %all-to-all-done.3 = bf16[32,1,4,384]{3,2,1,0:T(4,128)(2,1)S(1)} async-done(((bf16[32,1,4,384]{3,2,1,0:T(4,128)(2,1)}), bf16[32,1,4,384]{3,2,1,0:T(4,128)(2,1)S(1)}, u32[]{:S(2)}, u32[]{:S(2)}) %all-to-all-start.3) | async-done | bytes 98336 | tf_op jit(solution)/shard_map/all_to_all | solution.py:87
  296.2 6.7 %all_to_all.30 = bf16[4,8,1,4,384]{4,1,3,2,0:T(8,128)(2,1)S(1)} all-to-all(bf16[4,8,1,4,384]{4,1,3,2,0:T(8,128)(2,1)S(1)} %pad_maximum_fusion), channel_id=1, replica_groups=mesh['gz'=4,'gy'=4,'gx'=2] {'gz'}, dimensions={0} | all-to-all | bytes 196608 | tf_op jit(solution)/shard_map/all_to_all | solution.py:12
  (300 shorter events, 93.0 us)
Async XLA Ops:
  6.5 61.5 %all-gather.9.cloned.1.call-start = ((), (), s32[]{:S(2)}) async-start(), calls=%async_computation.6 | async-start | bytes 1622016 | tf_op jit(solution)/shard_map/all_gather | solution.py:54
  9.0 115.9 %all-gather.11.cloned.1.call-start = ((), (), s32[]{:S(2)}) async-start(), calls=%async_computation.7 | async-start | bytes 1622016 | tf_op jit(solution)/shard_map/all_gather | solution.py:54
  10.0 171.8 %all-gather.7.cloned.1.call-start = ((), (), s32[]{:S(2)}) async-start(), calls=%async_computation.5 | async-start | bytes 1622016 | tf_op jit(solution)/shard_map/all_gather | solution.py:54
  20.3 170.1 %copy-start.11 = (bf16[8,1,16,384]{3,0,1,2:T(8,128)(2,1)}, bf16[8,1,16,384]{3,0,1,2:T(8,128)(2,1)S(1)}, u32[]{:S(2)}) copy-start(bf16[8,1,16,384]{3,0,1,2:T(8,128)(2,1)S(1)} %all_to_all.29) | copy-start | bytes 294916
  20.3 171.1 %all-to-all-start = ((bf16[8,1,16,384]{3,2,1,0:T(8,128)(2,1)}), bf16[8,1,16,384]{3,2,1,0:T(8,128)(2,1)S(1)}, u32[]{:S(2)}, u32[]{:S(2)}) async-start(bf16[8,1,16,384]{3,2,1,0:T(8,128)(2,1)} %param.5), calls=%async_computation | async-start | bytes 196608 | tf_op jit(solution)/shard_map/all_to_all | solution.py:93
  74.0 9.7 %copy-start = (f32[1,32,4,6,64]{4,3,1,2,0:T(8,128)}, f32[1,32,4,6,64]{4,3,1,2,0:T(8,128)S(1)}, u32[]{:S(2)}) copy-start(f32[1,32,4,6,64]{4,3,1,2,0:T(8,128)S(1)} %reshape.969) | copy-start | bytes 589828
  84.0 41.0 %copy-start.16 = (f32[4,6,32,32]{2,3,1,0:T(8,128)}, f32[4,6,32,32]{2,3,1,0:T(8,128)S(1)}, u32[]{:S(2)}) copy-start(f32[4,6,32,32]{2,3,1,0:T(8,128)S(1)} %get-tuple-element.30) | copy-start | bytes 294916
  84.0 43.8 %copy-start.53 = (f32[4,6,32]{2,1,0:T(8,128)}, f32[4,6,32]{2,1,0:T(8,128)S(1)}, u32[]{:S(2)}) copy-start(f32[4,6,32]{2,1,0:T(8,128)S(1)} %get-tuple-element.29) | copy-start | bytes 9220
  186.6 3.5 %copy-start.38 = (bf16[1,32,4,6,64]{4,1,3,2,0:T(8,128)(2,1)S(1)}, bf16[1,32,4,6,64]{4,1,3,2,0:T(8,128)(2,1)}, u32[]{:S(2)}) copy-start(bf16[1,32,4,6,64]{4,1,3,2,0:T(8,128)(2,1)} %fusion.6) | copy-start | bytes 294916
  186.6 3.8 %copy-start.9 = (bf16[384,8,48]{0,2,1:T(8,128)(2,1)S(1)}, bf16[384,8,48]{0,2,1:T(8,128)(2,1)}, u32[]{:S(2)}) copy-start(bf16[384,8,48]{0,2,1:T(8,128)(2,1)} %slice.95) | copy-start | bytes 884740
  191.3 13.1 %copy-start.29 = (bf16[8,1,16,384]{3,2,1,0:T(8,128)(2,1)}, bf16[8,1,16,384]{3,2,1,0:T(8,128)(2,1)S(1)}, u32[]{:S(2)}) copy-start(bf16[8,1,16,384]{3,2,1,0:T(8,128)(2,1)S(1)} %all-to-all-done) | copy-start | bytes 294916
  191.3 11.1 %all-to-all-start.2 = ((bf16[32,1,4,384]{3,2,1,0:T(4,128)(2,1)}), bf16[32,1,4,384]{3,2,1,0:T(4,128)(2,1)S(1)}, u32[]{:S(2)}, u32[]{:S(2)}) async-start(bf16[32,1,4,384]{3,2,1,0:T(4,128)(2,1)} %copy.530), calls=%async_computation.2 | async-start | bytes 196608 | tf_op jit(solution)/shard_map/all_to_all | solution.py:76
  253.0 4.9 %copy-start.47 = (f32[4,32,6]{1,0,2:T(4,128)S(1)}, f32[4,32,6]{1,0,2:T(4,128)}, u32[]{:S(2)}) copy-start(f32[4,32,6]{1,0,2:T(4,128)} %copy.547) | copy-start | bytes 9220
  258.6 5.0 %copy-start.52 = (f32[4,32,6]{1,2,0:T(8,128)S(1)}, f32[4,32,6]{1,2,0:T(8,128)}, u32[]{:S(2)}) copy-start(f32[4,32,6]{1,2,0:T(8,128)} %copy.566) | copy-start | bytes 9220
  265.0 4.6 %copy-start.59 = (f32[4,32]{1,0:T(4,128)S(1)}, f32[4,32]{1,0:T(4,128)}, u32[]{:S(2)}) copy-start(f32[4,32]{1,0:T(4,128)} %copy-done.58) | copy-start | bytes 1540
  265.0 4.6 %copy-start.57 = (f32[4,32]{1,0:T(4,128)S(1)}, f32[4,32]{1,0:T(4,128)}, u32[]{:S(2)}) copy-start(f32[4,32]{1,0:T(4,128)} %copy-done.56) | copy-start | bytes 1540
  269.6 3.4 %copy-start.15 = (f32[32,6,4,4]{2,3,1,0:T(4,128)S(1)}, f32[32,6,4,4]{2,3,1,0:T(4,128)}, u32[]{:S(2)}) copy-start(f32[32,6,4,4]{2,3,1,0:T(4,128)} %copy-done.14) | copy-start | bytes 36868
  269.6 3.4 %copy-start.40 = (f32[32,6,4]{2,1,0:T(8,128)S(1)}, f32[32,6,4]{2,1,0:T(8,128)}, u32[]{:S(2)}) copy-start(f32[32,6,4]{2,1,0:T(8,128)} %multiply_divide_fusion) | copy-start | bytes 9220
  269.8 4.8 %copy-start.19 = (f32[32,6,4]{2,1,0:T(8,128)S(1)}, f32[32,6,4]{2,1,0:T(8,128)}, u32[]{:S(2)}) copy-start(f32[32,6,4]{2,1,0:T(8,128)} %copy-done.18) | copy-start | bytes 9220
  279.8 3.9 %copy-start.54 = (f32[4,6,32]{2,1,0:T(8,128)S(1)}, f32[4,6,32]{2,1,0:T(8,128)}, u32[]{:S(2)}) copy-start(f32[4,6,32]{2,1,0:T(8,128)} %copy-done.53) | copy-start | bytes 9220
  279.8 11.5 %copy-start.10 = (bf16[384,8,48]{0,2,1:T(8,128)(2,1)S(1)}, bf16[384,8,48]{0,2,1:T(8,128)(2,1)}, u32[]{:S(2)}) copy-start(bf16[384,8,48]{0,2,1:T(8,128)(2,1)} %slice.95) | copy-start | bytes 884740
  279.8 11.9 %copy-start.17 = (f32[4,6,32,32]{2,3,1,0:T(8,128)S(1)}, f32[4,6,32,32]{2,3,1,0:T(8,128)}, u32[]{:S(2)}) copy-start(f32[4,6,32,32]{2,3,1,0:T(8,128)} %copy-done.16) | copy-start | bytes 294916
  280.3 11.5 %copy-start.21 = (bf16[32,4,6,64]{3,2,0,1:T(8,128)(2,1)S(1)}, bf16[32,4,6,64]{3,2,0,1:T(8,128)(2,1)}, u32[]{:S(2)}) copy-start(bf16[32,4,6,64]{3,2,0,1:T(8,128)(2,1)} %convert_element_type.405) | copy-start | bytes 294916
  281.0 10.2 %all-to-all-start.3 = ((bf16[32,1,4,384]{3,2,1,0:T(4,128)(2,1)}), bf16[32,1,4,384]{3,2,1,0:T(4,128)(2,1)S(1)}, u32[]{:S(2)}, u32[]{:S(2)}) async-start(bf16[32,1,4,384]{3,2,1,0:T(4,128)(2,1)} %bitcast.70), calls=%async_computation.3 | async-start | bytes 196608 | tf_op jit(solution)/shard_map/all_to_all | solution.py:87
  (43 other events, 63.7 us)
Sparse Core Ops, SparseCore 0:
  10.2 57.8 all-gather.8
  71.0 53.9 all-gather.10
  127.9 53.9 all-gather.6
